TPU v7x, 512 devices: a whole 4x8x8 slice. The times are simulated.
512 devices in a mesh: section: 8 (over z), ctx: 8 (over y_hi, x), tp: 8 (over y_lo, core).
Axes of the slice: x: 4, y: 8 (y_hi: 2, y_lo: 4; y = y_hi * 4 + y_lo), z: 8, core: 2. Of those that a mesh axis runs over, the one named last changes fastest.
Arguments:
- block_order: int32 [16], replicated, may hold values from 0 to 15, each once
- plan: int32 [8], replicated, may hold values from 0 to 1
- q_box: bfloat16 [8, 2, 1408, 8192], P('section', None, 'ctx', 'tp'), may hold values from -8 to 8
- k_box: bfloat16 [8, 2, 1408, 1024], P('section', None, ('ctx', 'tp')), may hold values from -8 to 8
- v_box: bfloat16 [8, 2, 1408, 1024], P('section', None, ('ctx', 'tp')), may hold values from -6 to 6
- grad_out: bfloat16 [8, 1408, 8192], P('section', 'ctx', 'tp'), may hold values from -6 to 6
Outputs:
- attn_out: bfloat16 [8, 1408, 8192], P('section', 'ctx', 'tp')
- grad_q: bfloat16 [8, 1408, 8192], P('section', 'ctx', 'tp')
- grad_k: float32 [8, 1408, 1024], P('section', ('ctx', 'tp'))
- grad_v: float32 [8, 1408, 1024], P('section', ('ctx', 'tp'))
Inputs may be any that keep to these rules, and one draw needn't show every extreme that they name: `block_order`: a permutation: every block sits in exactly one storage slot, slot j covering storage rows j * 88 to (j + 1) * 88 - 1.
All inputs are finite; a program needn't handle non-finite values.
Results may differ from a plain program's by a relative error of at most 0.012.
Values may be sent and summed in bfloat16 or wider, within the bound.
No kernel may reach another device: no remote copies, remote signals or barrier semaphores. Data moves between devices by JAX's collectives and lax.ppermute only.
A program may use at most 64 MiB of HBM per device.

v0:
```python
import jax
import jax.numpy as jnp
from jax import lax
from jax.sharding import PartitionSpec as P

HEAD_DIM = 128
NEG = -1e30


def passed_along(block, axis, distance):
    devices = range(lax.axis_size(axis))
    route = [((i - distance) % len(devices), i) for i in devices]
    return lax.ppermute(block, axis, route)


def body(block_order, plan, q_box, k_box, v_box, grad_out):
    tp_count = lax.axis_size("tp")
    ctx_count = lax.axis_size("ctx")
    section_count = lax.axis_size("section")
    tok_rows = q_box.shape[2]
    kv_rows = k_box.shape[2]
    seq_rows = tok_rows * ctx_count
    block_len = seq_rows // block_order.shape[0]
    head_size = HEAD_DIM
    heads_local = q_box.shape[3] // head_size
    kv_local = k_box.shape[3] // head_size // tp_count
    group = heads_local // kv_local
    kv_width = kv_local * head_size
    scale = head_size ** (-0.5)
    section_rank = lax.axis_index("section")
    receiver = (section_rank + 1) % section_count
    wanted = lax.dynamic_index_in_dim(plan, receiver, 0, keepdims=False)
    q_send = lax.dynamic_index_in_dim(q_box[0], wanted, 0, keepdims=False)
    k_send = lax.dynamic_index_in_dim(k_box[0], wanted, 0, keepdims=False)
    v_send = lax.dynamic_index_in_dim(v_box[0], wanted, 0, keepdims=False)
    kv_send = jnp.stack(
        [k_send.reshape(kv_rows, -1, head_size), v_send.reshape(kv_rows, -1, head_size)], axis=2
    ).reshape(kv_rows, -1)
    queries, kv_rows_in = passed_along((q_send, kv_send), "section", 1)
    cotangent = passed_along(grad_out[0], "section", -1)
    kv_tok = lax.all_to_all(kv_rows_in, "tp", split_axis=1, concat_axis=0, tiled=True)
    kv_full = lax.all_gather(kv_tok, "ctx", axis=0, tiled=True)
    kv_full = kv_full.reshape(seq_rows, kv_local, 2, head_size)
    key_heads = kv_full[:, :, 0, :]
    value_heads = kv_full[:, :, 1, :]
    positions = (
        block_order[:, None] * block_len + jnp.arange(block_len, dtype=jnp.int32)[None, :]
    ).reshape(seq_rows)
    query_pos = lax.dynamic_slice_in_dim(positions, lax.axis_index("ctx") * tok_rows, tok_rows)
    visible = (positions[None, :] <= query_pos[:, None])[None, None]
    q4 = queries.reshape(tok_rows, kv_local, group, head_size)
    do4 = cotangent.reshape(tok_rows, kv_local, group, head_size)
    scores = jnp.einsum("qgjd,kgd->gjqk", q4, key_heads, preferred_element_type=jnp.float32) * scale
    scores = jnp.where(visible, scores, NEG)
    top_score = jnp.max(scores, axis=-1, keepdims=True)
    totals = jnp.sum(jnp.where(visible, jnp.exp(scores - top_score), 0.0), axis=-1, keepdims=True)
    log_total = top_score + jnp.log(totals)
    probs = jnp.where(visible, jnp.exp(scores - log_total), 0.0)
    probs_low = probs.astype(jnp.bfloat16)
    attended = jnp.einsum(
        "gjqk,kgd->qgjd", probs_low, value_heads, preferred_element_type=jnp.float32
    )
    delta = jnp.sum(do4.astype(jnp.float32) * attended, axis=-1)
    dprobs = jnp.einsum("qgjd,kgd->gjqk", do4, value_heads, preferred_element_type=jnp.float32)
    dscores = (probs * (dprobs - jnp.transpose(delta, (1, 2, 0))[..., None])).astype(jnp.bfloat16)
    q_grad = (
        jnp.einsum("gjqk,kgd->qgjd", dscores, key_heads, preferred_element_type=jnp.float32) * scale
    ).astype(jnp.bfloat16)
    key_grad = jnp.einsum("gjqk,qgjd->kgd", dscores, q4, preferred_element_type=jnp.float32) * scale
    value_grad = jnp.einsum("gjqk,qgjd->kgd", probs_low, do4, preferred_element_type=jnp.float32)
    attended_flat = attended.astype(jnp.bfloat16).reshape(tok_rows, heads_local * head_size)
    q_grad_flat = q_grad.reshape(tok_rows, heads_local * head_size)
    grad_terms = jnp.stack([key_grad, value_grad], axis=2).reshape(seq_rows, 2 * kv_width)
    own_grads = lax.psum_scatter(grad_terms, "ctx", scatter_dimension=0, tiled=True)
    tok_grads = lax.all_to_all(own_grads, "tp", split_axis=0, concat_axis=1, tiled=True)
    tok_grads = tok_grads.reshape(kv_rows, -1, 2, head_size)
    k_grad_tokens = tok_grads[:, :, 0, :].reshape(kv_rows, -1)
    v_grad_tokens = tok_grads[:, :, 1, :].reshape(kv_rows, -1)
    return (attended_flat[None], q_grad_flat[None], k_grad_tokens[None], v_grad_tokens[None])


def solution(mesh):
    in_specs = (
        P(),
        P(),
        P("section", None, "ctx", "tp"),
        P("section", None, ("ctx", "tp"), None),
        P("section", None, ("ctx", "tp"), None),
        P("section", "ctx", "tp"),
    )
    out_specs = (
        P("section", "ctx", "tp"),
        P("section", "ctx", "tp"),
        P("section", ("ctx", "tp"), None),
        P("section", ("ctx", "tp"), None),
    )
    return jax.shard_map(body, mesh=mesh, in_specs=in_specs, out_specs=out_specs, check_vma=False)
```

profile of v0, /device:TPU:1, one launch (start us, length us, event | category | flops | bytes accessed | tf_op | source)
XLA Modules:
  0.0 212.7 jit_solution(3541561579943129193)
XLA Ops:
  7.2 11.6 %collective-permute-start.2 = (bf16[176,1024]{1,0:T(8,128)(2,1)}, bf16[176,1024]{1,0:T(8,128)(2,1)S(1)}, u32[]{:S(2)}, u32[]{:S(2)}) collective-permute-start(bf16[176,1024]{1,0:T(8,128)(2,1)} %bitcast.163), channel_id=1, source_target_pairs={{64,0},{128,64},{192,128},{256,192},{320,256},{384,320},{448,384},... | collective-permute-start | bytes 1081352 | tf_op jit(solution)/shard_map/ppermute | solution.py:13
  18.8 1.2 dynamic_slice.18
  22.0 1.5 dynamic-slice_reduce_fusion
  23.7 1.9 collective-permute-start
  25.6 0.8 dynamic-slice_bitcast_fusion
  26.4 1.9 collective-permute-start.1
  28.3 0.7 broadcast_multiply_fusion
  29.2 1.0 collective-permute-done
  30.3 0.7 copy.27
  31.0 7.0 %all-to-all-start = ((bf16[22,8,256]{2,0,1:T(8,128)(2,1)}), bf16[22,8,256]{2,0,1:T(8,128)(2,1)S(1)}, u32[]{:S(2)}, u32[]{:S(2)}) async-start(bf16[22,8,256]{2,0,1:T(8,128)(2,1)} %copy.27), calls=%async_computation | async-start | bytes 196608 | tf_op jit(solution)/shard_map/all_to_all | solution.py:41
  37.9 0.2 broadcast_compare_fusion
  38.2 5.1 %all-to-all-done = bf16[22,8,256]{2,0,1:T(8,128)(2,1)S(1)} async-done(((bf16[22,8,256]{2,0,1:T(8,128)(2,1)}), bf16[22,8,256]{2,0,1:T(8,128)(2,1)S(1)}, u32[]{:S(2)}, u32[]{:S(2)}) %all-to-all-start) | async-done | bytes 90144 | tf_op jit(solution)/shard_map/all_to_all | solution.py:41
  43.3 41.5 %all_gather.3 = bf16[1408,256]{1,0:T(8,128)(2,1)S(1)} all-gather(bf16[176,256]{1,0:T(8,128)(2,1)S(1)} %all_to_all.29), channel_id=1, replica_groups=mesh['section'=8,'ctx'=8,'tp'=8] {'ctx'}, dimensions={0}, use_global_device_ids=true | all-gather | bytes 811008 | tf_op jit(solution)/shard_map/all_gather | solution.py:42
  84.9 0.3 copy.28
  85.3 0.1 copy.47
  85.4 2.0 fusion.30
  87.4 2.0 select_reduce_fusion
  89.5 1.8 fusion.18
  91.3 2.7 %fusion.6 = bf16[8,176,1408]{2,1,0:T(8,128)(2,1)S(1)} fusion(f32[8,176]{1,0:T(8,128)S(1)} %bitcast.162, f32[1,8,176,1408]{3,2,1,0:T(8,128)S(1)} %get-tuple-element.13, f32[8,176]{1,0:T(8,128)S(1)} %log_add_fusion, pred[176,1408]{1,0:T(8,128)(4,1)S(1)} %broadcast_compare_fusion, bf16[1408,1,2,128]{0,3,2,1:T(8,128)(2,1)S(1)} %bitcast.146, ...), kind=kOutput, calls=%fused_computation.10 | convolution fusion | flops 517423104 | bytes 12879872 | tf_op jit(solution)/shard_map/qgjd,kgd->gjqk/dot_general | solution.py:64
  94.0 0.9 fusion.13
  94.9 1.7 convolution_bitcast_fusion
  96.6 0.1 pad_maximum_fusion
  96.7 1.5 copy.38
  98.2 0.1 copy.32
  98.3 0.9 broadcast_in_dim_reshape.7
  99.2 90.8 %reduce-scatter.2.cloned.1.call-done = f32[176,256]{1,0:T(8,128)} async-done(((f32[1408,256]{1,0:T(8,128)}), f32[176,256]{1,0:T(8,128)}) %reduce-scatter.2.cloned.1.call-update) | async-done | bytes 180240 | tf_op jit(solution)/shard_map/reduce_scatter | solution.py:74
  190.0 1.6 all_to_all.30
  191.6 7.0 %all-to-all-start.1 = ((f32[8,22,256]{2,1,0:T(8,128)}), f32[8,22,256]{2,1,0:T(8,128)S(1)}, u32[]{:S(2)}, u32[]{:S(2)}) async-start(f32[8,22,256]{2,1,0:T(8,128)} %all_to_all.30), calls=%async_computation.2 | async-start | bytes 393216 | tf_op jit(solution)/shard_map/all_to_all | solution.py:75
  198.6 3.3 %fusion.17 = bf16[176,1,8,128]{3,0,2,1:T(8,128)(2,1)S(1)} fusion(bf16[8,176,1408]{2,1,0:T(8,128)(2,1)} %copy-done.1, bf16[1408,1,2,128]{0,3,2,1:T(8,128)(2,1)S(1)} %bitcast.147), kind=kOutput, calls=%fused_computation.19 | convolution fusion | flops 507871232 | bytes 4685824 | tf_op jit(solution)/shard_map/gjqk,kgd->qgjd/dot_general | solution.py:67
  202.0 0.9 broadcast_in_dim_reshape.8
  202.9 2.2 %all-to-all-done.1 = f32[8,22,256]{2,1,0:T(8,128)S(1)} async-done(((f32[8,22,256]{2,1,0:T(8,128)}), f32[8,22,256]{2,1,0:T(8,128)S(1)}, u32[]{:S(2)}, u32[]{:S(2)}) %all-to-all-start.1) | async-done | bytes 180256 | tf_op jit(solution)/shard_map/all_to_all | solution.py:75
  205.2 0.7 fusion.29
  (26 shorter events, 0.8 us)
Async XLA Ops:
  7.2 18.5 %copy-start = (bf16[1,2,176,1024]{3,2,1,0:T(8,128)(2,1)S(1)}, bf16[1,2,176,1024]{3,2,1,0:T(8,128)(2,1)}, u32[]{:S(2)}) copy-start(bf16[1,2,176,1024]{3,2,1,0:T(8,128)(2,1)} %param.8) | copy-start | bytes 2162692
  7.2 78.0 %collective-permute-start.2 = (bf16[176,1024]{1,0:T(8,128)(2,1)}, bf16[176,1024]{1,0:T(8,128)(2,1)S(1)}, u32[]{:S(2)}, u32[]{:S(2)}) collective-permute-start(bf16[176,1024]{1,0:T(8,128)(2,1)} %bitcast.163), channel_id=1, source_target_pairs={{64,0},{128,64},{192,128},{256,192},{320,256},{384,320},{448,384},... | collective-permute-start | bytes 1081352 | tf_op jit(solution)/shard_map/ppermute | solution.py:13
  23.7 6.6 %collective-permute-start = (bf16[22,2048]{1,0:T(8,128)(2,1)S(1)}, bf16[22,2048]{1,0:T(8,128)(2,1)S(1)}, u32[]{:S(2)}, u32[]{:S(2)}) collective-permute-start(bf16[22,2048]{1,0:T(8,128)(2,1)S(1)} %reshape.167), channel_id=1, source_target_pairs={{448,0},{0,64},{64,128},{128,192},{192,256},{256,320},{320,384},{3... | collective-permute-start | bytes 270344 | tf_op jit(solution)/shard_map/ppermute | solution.py:13
  26.4 59.0 %collective-permute-start.1 = (bf16[176,1024]{1,0:T(8,128)(2,1)}, bf16[176,1024]{1,0:T(8,128)(2,1)S(1)}, u32[]{:S(2)}, u32[]{:S(2)}) collective-permute-start(bf16[176,1024]{1,0:T(8,128)(2,1)} %dynamic-slice_bitcast_fusion), channel_id=1, source_target_pairs={{448,0},{0,64},{64,128},{128,192},{192,256},{256,320},{320,384},{3... | collective-permute-start | bytes 1081352 | tf_op jit(solution)/shard_map/ppermute | solution.py:13
  31.0 12.3 %all-to-all-start = ((bf16[22,8,256]{2,0,1:T(8,128)(2,1)}), bf16[22,8,256]{2,0,1:T(8,128)(2,1)S(1)}, u32[]{:S(2)}, u32[]{:S(2)}) async-start(bf16[22,8,256]{2,0,1:T(8,128)(2,1)} %copy.27), calls=%async_computation | async-start | bytes 196608 | tf_op jit(solution)/shard_map/all_to_all | solution.py:41
  37.9 152.1 %reduce-scatter.2.cloned.1.call-start = ((), (), s32[]{:S(2)}) async-start(), calls=%async_computation.3 | async-start | bytes 1622016 | tf_op jit(solution)/shard_map/reduce_scatter | solution.py:74
  94.0 2.6 %copy-start.1 = (bf16[8,176,1408]{2,1,0:T(8,128)(2,1)}, bf16[8,176,1408]{2,1,0:T(8,128)(2,1)S(1)}, u32[]{:S(2)}) copy-start(bf16[8,176,1408]{2,1,0:T(8,128)(2,1)S(1)} %fusion.6) | copy-start | bytes 11894788
  191.6 13.5 %all-to-all-start.1 = ((f32[8,22,256]{2,1,0:T(8,128)}), f32[8,22,256]{2,1,0:T(8,128)S(1)}, u32[]{:S(2)}, u32[]{:S(2)}) async-start(f32[8,22,256]{2,1,0:T(8,128)} %all_to_all.30), calls=%async_computation.2 | async-start | bytes 393216 | tf_op jit(solution)/shard_map/all_to_all | solution.py:75
Sparse Core Ops, SparseCore 0:
  98.4 91.6 reduce-scatter.1
where the time goes:
time: 213 us
  waiting for transfers between devices  99.2 us (47%)
  blocking collectives  41.5 us (19%)
  starting transfers between devices  29.4 us (14%)
  between operations  16.2 us (8%)
  matrix products  12.3 us (6%)
  local copies, waits for them, and re-layouts  10.9 us (5%)
  other arithmetic  3.13 us (1%)
    reduce_scatter x1, waiting for transfers between devices, body(): lax.psum_scatter(grad_terms, 'ctx', scatter_dimension=0, tiled=True)  90.8 us
    all_gather x1, blocking collectives, body(): kv_full = lax.all_gather(kv_tok, 'ctx', axis=0, tiled=True)  41.5 us
    ppermute x3, starting transfers between devices, passed_along(): return lax.ppermute(block, axis, route)  15.4 us
    all_to_all x1, starting transfers between devices, body(): lax.all_to_all(kv_rows_in, 'tp', split_axis=1, concat_axis=0, tiled=True)  6.98 us
    all_to_all x1, starting transfers between devices, body(): lax.all_to_all(own_grads, 'tp', split_axis=0, concat_axis=1, tiled=True)  6.96 us
    all_to_all x1, waiting for transfers between devices, body(): lax.all_to_all(kv_rows_in, 'tp', split_axis=1, concat_axis=0, tiled=True)  5.15 us
  transfers between devices with their start and end apart: 6, of which 4 were waited for; matrix products, arithmetic and copies ran while one was open for 5% of the time, Pallas kernels for 0%

commit v1 on v0

--- a/solution.py
+++ b/solution.py
@@ -72,7 +72,20 @@
     q_grad_flat = q_grad.reshape(tok_rows, heads_local * head_size)
     grad_terms = jnp.stack([key_grad, value_grad], axis=2).reshape(seq_rows, 2 * kv_width)
     own_grads = lax.psum_scatter(grad_terms, "ctx", scatter_dimension=0, tiled=True)
-    tok_grads = lax.all_to_all(own_grads, "tp", split_axis=0, concat_axis=1, tiled=True)
+
+    def build_types(pos_dim, dim_no, mesh_name, vec):
+        big = jnp.concatenate(
+            jax.lax.all_to_all(
+                jnp.stack(jnp.split(vec, jax.lax.axis_size(mesh_name), dim_no), axis=0),
+                mesh_name,
+                0,
+                0,
+            ),
+            pos_dim,
+        )
+        return big
+
+    tok_grads = build_types(1, 0, "tp", vec=own_grads)
     tok_grads = tok_grads.reshape(kv_rows, -1, 2, head_size)
     k_grad_tokens = tok_grads[:, :, 0, :].reshape(kv_rows, -1)
     v_grad_tokens = tok_grads[:, :, 1, :].reshape(kv_rows, -1)

time: 213 us -> 215 us (level)
    reduce_scatter x1 -> x0, waiting for transfers between devices: 90.8 us -> none  [body(): lax.psum_scatter(grad_terms, 'ctx', scatter_dimension=0, tiled=True)]
    unnamed x1 -> x2, waiting for transfers between devices: 0.02 us -> 90.8 us
    unnamed x9 -> x25, local copies, waits for them, and re-layouts: 0.24 us -> 2.77 us
where the time goes in v1:
time: 215 us; the launch traced here: 214 us
  waiting for transfers between devices  99.2 us (46%)
  blocking collectives  41.5 us (19%)
  starting transfers between devices  29.4 us (14%)
  between operations  16.3 us (8%)
  matrix products  12.3 us (6%)
  local copies, waits for them, and re-layouts  12.2 us (6%)
  other arithmetic  3.13 us (1%)
    unnamed x2, waiting for transfers between devices  90.8 us
    all_gather x1, blocking collectives, body(): kv_full = lax.all_gather(kv_tok, 'ctx', axis=0, tiled=True)  41.5 us
    ppermute x3, starting transfers between devices, passed_along(): return lax.ppermute(block, axis, route)  15.4 us
    all_to_all x1, starting transfers between devices, body(): lax.all_to_all(kv_rows_in, 'tp', split_axis=1, concat_axis=0, tiled=True)  6.98 us
    all_to_all x1, starting transfers between devices, build_types(): jax.lax.all_to_all(jnp.stack(jnp.split(vec, jax.lax.axis_size(mesh_name),...  6.96 us
    all_to_all x1, waiting for transfers between devices, body(): lax.all_to_all(kv_rows_in, 'tp', split_axis=1, concat_axis=0, tiled=True)  5.15 us
  transfers between devices with their start and end apart: 6, of which 4 were waited for; matrix products, arithmetic and copies ran while one was open for 5% of the time, Pallas kernels for 0%

profile of v1, /device:TPU:1, one launch (start us, length us, event | category | flops | bytes accessed | tf_op | source)
XLA Modules:
  0.0 214.1 jit_solution(7100270074335350858)
XLA Ops:
  7.2 11.6 %collective-permute-start.2 = (bf16[176,1024]{1,0:T(8,128)(2,1)}, bf16[176,1024]{1,0:T(8,128)(2,1)S(1)}, u32[]{:S(2)}, u32[]{:S(2)}) collective-permute-start(bf16[176,1024]{1,0:T(8,128)(2,1)} %bitcast.180), channel_id=1, source_target_pairs={{64,0},{128,64},{192,128},{256,192},{320,256},{384,320},{448,384},... | collective-permute-start | bytes 1081352 | tf_op jit(solution)/shard_map/ppermute | solution.py:13
  18.8 1.2 dynamic_slice.18
  22.0 1.5 dynamic-slice_reduce_fusion
  23.7 1.9 collective-permute-start
  25.6 0.8 dynamic-slice_bitcast_fusion
  26.4 1.9 collective-permute-start.1
  28.3 0.7 broadcast_multiply_fusion
  29.2 1.0 collective-permute-done
  30.3 0.7 copy.96
  31.0 7.0 %all-to-all-start = ((bf16[22,8,256]{2,0,1:T(8,128)(2,1)}), bf16[22,8,256]{2,0,1:T(8,128)(2,1)S(1)}, u32[]{:S(2)}, u32[]{:S(2)}) async-start(bf16[22,8,256]{2,0,1:T(8,128)(2,1)} %copy.96), calls=%async_computation | async-start | bytes 196608 | tf_op jit(solution)/shard_map/all_to_all | solution.py:41
  37.9 0.2 broadcast_compare_fusion
  38.2 5.1 %all-to-all-done = bf16[22,8,256]{2,0,1:T(8,128)(2,1)S(1)} async-done(((bf16[22,8,256]{2,0,1:T(8,128)(2,1)}), bf16[22,8,256]{2,0,1:T(8,128)(2,1)S(1)}, u32[]{:S(2)}, u32[]{:S(2)}) %all-to-all-start) | async-done | bytes 90144 | tf_op jit(solution)/shard_map/all_to_all | solution.py:41
  43.3 41.5 %all_gather.3 = bf16[1408,256]{1,0:T(8,128)(2,1)S(1)} all-gather(bf16[176,256]{1,0:T(8,128)(2,1)S(1)} %all_to_all.20), channel_id=1, replica_groups=mesh['section'=8,'ctx'=8,'tp'=8] {'ctx'}, dimensions={0}, use_global_device_ids=true | all-gather | bytes 811008 | tf_op jit(solution)/shard_map/all_gather | solution.py:42
  84.9 0.3 copy.97
  85.3 0.1 copy.126
  85.4 2.0 fusion.31
  87.4 2.0 select_reduce_fusion
  89.5 1.8 fusion.18
  91.3 2.7 %fusion.6 = bf16[8,176,1408]{2,1,0:T(8,128)(2,1)S(1)} fusion(f32[8,176]{1,0:T(8,128)S(1)} %bitcast.179, f32[1,8,176,1408]{3,2,1,0:T(8,128)S(1)} %get-tuple-element.21, f32[8,176]{1,0:T(8,128)S(1)} %log_add_fusion, pred[176,1408]{1,0:T(8,128)(4,1)S(1)} %broadcast_compare_fusion, bf16[1408,1,2,128]{0,3,2,1:T(8,128)(2,1)S(1)} %bitcast.164, ...), kind=kOutput, calls=%fused_computation.10 | convolution fusion | flops 517423104 | bytes 12879872 | tf_op jit(solution)/shard_map/qgjd,kgd->gjqk/dot_general | solution.py:64
  94.0 0.9 fusion.13
  94.9 1.7 convolution_bitcast_fusion
  96.7 1.5 copy.109
  98.3 0.9 broadcast_in_dim_reshape.7
  99.2 90.8 %reduce-scatter.4.cloned.1.call-done = f32[176,256]{1,0:T(8,128)} async-done(((f32[1408,256]{1,0:T(8,128)}), f32[176,256]{1,0:T(8,128)}) %reduce-scatter.4.cloned.1.call-update) | async-done | bytes 180240
  190.0 0.9 fusion.30
  190.9 0.1 copy.113
  192.0 1.0 copy.107
  193.0 7.0 %all-to-all-start.1 = ((f32[8,22,256]{2,1,0:T(8,128)}), f32[8,22,256]{2,1,0:T(8,128)S(1)}, u32[]{:S(2)}, u32[]{:S(2)}) async-start(f32[8,22,256]{2,1,0:T(8,128)} %copy.107), calls=%async_computation.1 | async-start | bytes 393216 | tf_op jit(solution)/shard_map/all_to_all | solution.py:78
  200.0 3.3 %fusion.17 = bf16[176,1,8,128]{3,0,2,1:T(8,128)(2,1)S(1)} fusion(bf16[8,176,1408]{2,1,0:T(8,128)(2,1)} %copy-done.1, bf16[1408,1,2,128]{0,3,2,1:T(8,128)(2,1)S(1)} %bitcast.165), kind=kOutput, calls=%fused_computation.19 | convolution fusion | flops 507871232 | bytes 4685824 | tf_op jit(solution)/shard_map/gjqk,kgd->qgjd/dot_general | solution.py:67
  203.4 0.9 broadcast_in_dim_reshape.8
  204.3 2.2 %all-to-all-done.1 = f32[8,22,256]{2,1,0:T(8,128)S(1)} async-done(((f32[8,22,256]{2,1,0:T(8,128)}), f32[8,22,256]{2,1,0:T(8,128)S(1)}, u32[]{:S(2)}, u32[]{:S(2)}) %all-to-all-start.1) | async-done | bytes 180256 | tf_op jit(solution)/shard_map/all_to_all | solution.py:78
  206.6 0.7 fusion.29
  (43 shorter events, 1.9 us)
Async XLA Ops:
  7.2 18.5 %copy-start = (bf16[1,2,176,1024]{3,2,1,0:T(8,128)(2,1)S(1)}, bf16[1,2,176,1024]{3,2,1,0:T(8,128)(2,1)}, u32[]{:S(2)}) copy-start(bf16[1,2,176,1024]{3,2,1,0:T(8,128)(2,1)} %param.8) | copy-start | bytes 2162692
  7.2 78.0 %collective-permute-start.2 = (bf16[176,1024]{1,0:T(8,128)(2,1)}, bf16[176,1024]{1,0:T(8,128)(2,1)S(1)}, u32[]{:S(2)}, u32[]{:S(2)}) collective-permute-start(bf16[176,1024]{1,0:T(8,128)(2,1)} %bitcast.180), channel_id=1, source_target_pairs={{64,0},{128,64},{192,128},{256,192},{320,256},{384,320},{448,384},... | collective-permute-start | bytes 1081352 | tf_op jit(solution)/shard_map/ppermute | solution.py:13
  23.7 6.6 %collective-permute-start = (bf16[22,2048]{1,0:T(8,128)(2,1)S(1)}, bf16[22,2048]{1,0:T(8,128)(2,1)S(1)}, u32[]{:S(2)}, u32[]{:S(2)}) collective-permute-start(bf16[22,2048]{1,0:T(8,128)(2,1)S(1)} %reshape.163), channel_id=1, source_target_pairs={{448,0},{0,64},{64,128},{128,192},{192,256},{256,320},{320,384},{3... | collective-permute-start | bytes 270344 | tf_op jit(solution)/shard_map/ppermute | solution.py:13
  26.4 59.0 %collective-permute-start.1 = (bf16[176,1024]{1,0:T(8,128)(2,1)}, bf16[176,1024]{1,0:T(8,128)(2,1)S(1)}, u32[]{:S(2)}, u32[]{:S(2)}) collective-permute-start(bf16[176,1024]{1,0:T(8,128)(2,1)} %dynamic-slice_bitcast_fusion), channel_id=1, source_target_pairs={{448,0},{0,64},{64,128},{128,192},{192,256},{256,320},{320,384},{3... | collective-permute-start | bytes 1081352 | tf_op jit(solution)/shard_map/ppermute | solution.py:13
  31.0 12.3 %all-to-all-start = ((bf16[22,8,256]{2,0,1:T(8,128)(2,1)}), bf16[22,8,256]{2,0,1:T(8,128)(2,1)S(1)}, u32[]{:S(2)}, u32[]{:S(2)}) async-start(bf16[22,8,256]{2,0,1:T(8,128)(2,1)} %copy.96), calls=%async_computation | async-start | bytes 196608 | tf_op jit(solution)/shard_map/all_to_all | solution.py:41
  37.9 152.1 %reduce-scatter.4.cloned.1.call-start = ((), (), s32[]{:S(2)}) async-start(), calls=%async_computation.3 | async-start | bytes 1622016
  94.0 2.6 %copy-start.1 = (bf16[8,176,1408]{2,1,0:T(8,128)(2,1)}, bf16[8,176,1408]{2,1,0:T(8,128)(2,1)S(1)}, u32[]{:S(2)}) copy-start(bf16[8,176,1408]{2,1,0:T(8,128)(2,1)S(1)} %fusion.6) | copy-start | bytes 11894788
  193.0 13.5 %all-to-all-start.1 = ((f32[8,22,256]{2,1,0:T(8,128)}), f32[8,22,256]{2,1,0:T(8,128)S(1)}, u32[]{:S(2)}, u32[]{:S(2)}) async-start(f32[8,22,256]{2,1,0:T(8,128)} %copy.107), calls=%async_computation.1 | async-start | bytes 393216 | tf_op jit(solution)/shard_map/all_to_all | solution.py:78
Sparse Core Ops, SparseCore 0:
  98.4 91.6 reduce-scatter.3
